TPU v7x, 512 devices: a whole 4x4x16 slice. The times are simulated.
512 devices in a mesh: heads: 8 (over y, core), seq: 64 (over z, x).
Axes of the slice: x: 4, y: 4, z: 16, core: 2. Of those that a mesh axis runs over, the one named last changes fastest.
Arguments:
- query_proj: bfloat16 [8192, 4096], P('seq', 'heads'), may hold values from -6 to 6
- key_proj: bfloat16 [8192, 4096], P('seq', 'heads'), may hold values from -6 to 6
- value_proj: bfloat16 [8192, 4096], P('seq', 'heads'), may hold values from -6 to 6
- gate_proj: bfloat16 [8192, 4096], P('seq', 'heads'), may hold values from -6 to 6
- write_rate: float32 [32, 8192], P('heads', 'seq'), may hold values from 0 to 1
- log_decay: float32 [32, 8192], P('heads', 'seq'), may hold values from -1 to 0
- doc_start: int32 [8192], P('seq'), may hold values from 0 to 1, as said below
- norm_gain: float32 [128], replicated, may hold values from 0.5 to 1.5
- out_weight: bfloat16 [4096, 4096], P('heads', 'seq'), may hold values from -0.09375 to 0.09375
Outputs:
- layer_out: bfloat16 [8192, 4096], P('seq', 'heads')
Inputs may be any that keep to these rules, and one draw needn't show every extreme that they name: `doc_start`: exactly two entries are 1: one in the first half of the sequence (never token 0) and one in the second half.
All inputs are finite; a program needn't handle non-finite values.
Results may differ from a plain program's by a relative error of at most 0.017.
Values may be sent and summed in bfloat16 or wider, within the bound.
No kernel may reach another device: no remote copies, remote signals or barrier semaphores. Data moves between devices by JAX's collectives and lax.ppermute only.
A program may use at most 128 MiB of HBM per device.

v0:
```python
import jax
import jax.numpy as jnp
from jax import lax
from jax.sharding import Mesh
from jax.sharding import PartitionSpec as P

STRETCH = 64
SEQ_MINOR = 4
precise = lax.Precision.HIGHEST
epsilon = 1e-06


def unit_rows(block):
    return block / jnp.sqrt(jnp.sum(block * block, axis=-1, keepdims=True) + epsilon)


def triangular_inverse_below(system, right_side):
    return jax.scipy.linalg.solve_triangular(system, right_side, lower=True, unit_diagonal=True)


def matrix_product(left_side, right_side):
    return jnp.einsum("...de,...ef->...df", left_side, right_side, precision=precise)


def stretch_terms(queries, keys_normed, values_in, rates, decays, resets):
    length = queries.shape[-2]
    value_width = values_in.shape[-1]
    cumulated = jnp.cumsum(decays, axis=-1)
    seen = jnp.cumsum(resets, axis=-1)
    row_index = lax.broadcasted_iota(jnp.int32, (length, length), 0)
    col_index = lax.broadcasted_iota(jnp.int32, (length, length), 1)
    same_span = (seen[..., :, None] == seen[..., None, :]) & (row_index >= col_index)
    log_gap = jnp.where(same_span, cumulated[..., :, None] - cumulated[..., None, :], 0.0)
    pair_decay = jnp.where(same_span, jnp.exp(log_gap), 0.0)
    head_decay = jnp.exp(cumulated) * (seen == 0).astype(jnp.float32)
    tail_decay = jnp.exp(cumulated[..., -1:] - cumulated) * (seen[..., -1:] == seen).astype(
        jnp.float32
    )
    key_gram = jnp.einsum("...cd,...md->...cm", keys_normed, keys_normed, precision=precise)
    strict_part = jnp.where(row_index > col_index, rates[..., :, None] * pair_decay * key_gram, 0.0)
    system = strict_part + jnp.eye(length, dtype=jnp.float32)
    both_sides = jnp.concatenate(
        [rates[..., None] * values_in, (rates * head_decay)[..., None] * keys_normed], axis=-1
    )
    solved = triangular_inverse_below(system, both_sides)
    pseudo_values = solved[..., :value_width]
    key_weights = solved[..., value_width:]
    scores = pair_decay * jnp.einsum("...cd,...md->...cm", queries, keys_normed, precision=precise)
    query_state = head_decay[..., None] * queries - jnp.einsum(
        "...cm,...md->...cd", scores, key_weights, precision=precise
    )
    local_out = jnp.einsum("...cm,...md->...cd", scores, pseudo_values, precision=precise)
    identity = jnp.eye(keys_normed.shape[-1], dtype=jnp.float32)
    transit = head_decay[..., -1][..., None, None] * identity - jnp.einsum(
        "...cd,...ce->...de", keys_normed, tail_decay[..., None] * key_weights, precision=precise
    )
    written = jnp.einsum(
        "...cd,...ce->...de", keys_normed, tail_decay[..., None] * pseudo_values, precision=precise
    )
    return (query_state, local_out, transit, written)


def gated_norm(core_out, gate_block, gain):
    scale = lax.rsqrt(jnp.mean(core_out * core_out, axis=-1, keepdims=True) + epsilon)
    gate_float = gate_block.astype(jnp.float32)
    return (core_out * scale * gain * jax.nn.silu(gate_float)).astype(jnp.bfloat16)


def shift_down(array, step, fill):
    head = jnp.broadcast_to(fill, (step,) + array.shape[1:]).astype(array.dtype)
    return jnp.concatenate([head, array[:-step]], axis=0)


def on_device(
    query_proj,
    key_proj,
    value_proj,
    gate_proj,
    write_rate,
    log_decay,
    doc_start,
    norm_gain,
    out_weight,
    minor,
    major,
):
    head_count = write_rate.shape[0]
    key_width = query_proj.shape[1] // head_count
    value_width = value_proj.shape[1] // head_count

    def spread(array):
        return lax.all_to_all(array, "x", 1, 0, tiled=True)

    query_here = spread(query_proj)
    key_here = spread(key_proj)
    value_here = spread(value_proj)
    gate_here = spread(gate_proj)
    rates_here = lax.all_to_all(write_rate, "x", 0, 1, tiled=True)
    decays_here = lax.all_to_all(log_decay, "x", 0, 1, tiled=True)
    resets_here = lax.all_gather(doc_start, "x", tiled=True)
    tok_rows = query_here.shape[0]
    local_heads = head_count // minor
    blocks = tok_rows // STRETCH

    def stretch_major(array, width):
        return array.reshape(blocks, STRETCH, local_heads, width).transpose(0, 2, 1, 3)

    queries = unit_rows(stretch_major(query_here, key_width).astype(jnp.float32))
    keys_normed = unit_rows(stretch_major(key_here, key_width).astype(jnp.float32))
    values_in = stretch_major(value_here, value_width).astype(jnp.float32)
    rates = rates_here.reshape(local_heads, blocks, STRETCH).transpose(1, 0, 2)
    decays = decays_here.reshape(local_heads, blocks, STRETCH).transpose(1, 0, 2)
    resets = resets_here.reshape(blocks, 1, STRETCH)
    query_state, local_out, transit, written = stretch_terms(
        queries, keys_normed, values_in, rates, decays, resets
    )
    identity = jnp.eye(key_width, dtype=jnp.float32)
    reach, saved = (transit, written)
    step = 1
    while step < blocks:
        earlier_reach = shift_down(reach, step, identity)
        earlier_saved = shift_down(saved, step, 0.0)
        saved = matrix_product(reach, earlier_saved) + saved
        reach = matrix_product(reach, earlier_reach)
        step *= 2
    place = lax.axis_index("z")
    group_reach, group_saved = (reach[-1], saved[-1])
    step = 1
    while step < major:
        pairs = [(i, i + step) for i in range(major - step)]
        if 2 * step < major:
            got = lax.ppermute(jnp.stack([group_reach, group_saved]), "z", pairs)
            got_reach, got_saved = (got[0], got[1])
            new_saved = matrix_product(group_reach, got_saved) + group_saved
            group_reach = jnp.where(
                place >= step, matrix_product(group_reach, got_reach), group_reach
            )
        else:
            got_saved = lax.ppermute(group_saved, "z", pairs)
            new_saved = matrix_product(group_reach, got_saved) + group_saved
        group_saved = new_saved
        step *= 2
    incoming = lax.ppermute(group_saved, "z", [(i, i + 1) for i in range(major - 1)])
    entry_reach = shift_down(reach, 1, identity)
    entry_saved = shift_down(saved, 1, 0.0)
    entry_state = matrix_product(entry_reach, incoming[None]) + entry_saved
    core_out = (
        jnp.einsum("bhcd,bhde->bhce", query_state, entry_state, precision=precise) + local_out
    )
    core_tokens = core_out.transpose(0, 2, 1, 3).reshape(tok_rows, local_heads, value_width)
    normed = gated_norm(
        core_tokens, gate_here.reshape(tok_rows, local_heads, value_width), norm_gain
    )
    normed = normed.reshape(tok_rows, local_heads * value_width)
    normed = lax.all_to_all(normed, "x", 0, 1, tiled=True)
    partial_value = jnp.dot(
        normed,
        lax.all_gather(out_weight, ("z", "x"), axis=1, tiled=True),
        preferred_element_type=jnp.float32,
    )
    return lax.psum_scatter(
        partial_value.astype(jnp.bfloat16), "heads", scatter_dimension=1, tiled=True
    )


def solution(mesh):
    heads_size, seq_size = mesh.devices.shape
    minor = SEQ_MINOR
    major = seq_size // minor
    split_mesh = Mesh(mesh.devices.reshape(heads_size, major, minor), ("heads", "z", "x"))
    seq = ("z", "x")
    placed = (
        P(seq, "heads"),
        P(seq, "heads"),
        P(seq, "heads"),
        P(seq, "heads"),
        P("heads", seq),
        P("heads", seq),
        P(seq),
        P(),
        P("heads", seq),
    )

    def body(*arrays):
        return on_device(*arrays, minor=minor, major=major)

    return jax.shard_map(
        body, mesh=split_mesh, in_specs=placed, out_specs=P(seq, "heads"), check_vma=False
    )
```

profile of v0, /device:TPU:4, one launch (start us, length us, event | category | flops | bytes accessed | tf_op | source)
XLA Modules:
  0.0 234.6 jit_solution(6820988842869189103)
XLA Ops:
  6.5 9.2 %all-to-all-start = ((f32[4,1,128]{2,1,0:T(1,128)}), f32[4,1,128]{2,1,0:T(1,128)S(1)}, u32[]{:S(2)}, u32[]{:S(2)}) async-start(f32[4,1,128]{2,1,0:T(1,128)} %bitcast.231), calls=%async_computation | async-start | bytes 4096 | tf_op jit(solution)/shard_map/all_to_all | solution.py:99
  15.7 0.7 all-gather.3.cloned.1.call-update
  16.5 0.7 copy_bitcast_fusion.1
  17.2 7.7 %all-gather = s32[4,1,128]{2,1,0:T(1,128)S(1)} all-gather(s32[1,1,128]{2,1,0:T(1,128)} %bitcast.233), channel_id=1, replica_groups=mesh['heads'=8,'z'=16,'x'=4] {'x'}, dimensions={0}, use_global_device_ids=true | all-gather | bytes 2560 | tf_op jit(solution)/shard_map/all_gather | solution.py:100
  24.8 0.5 broadcast.246
  25.3 0.7 reduce.24
  26.4 1.6 copy_bitcast_fusion
  28.2 1.0 copy.59
  29.2 0.8 copy.60
  29.9 1.7 copy.69
  31.6 5.9 %all-to-all-start.3 = ((f32[4,1,128]{2,1,0:T(1,128)}), f32[4,1,128]{2,1,0:T(1,128)S(1)}, u32[]{:S(2)}, u32[]{:S(2)}) async-start(f32[4,1,128]{2,1,0:T(1,128)} %bitcast.232), calls=%async_computation.3 | async-start | bytes 4096 | tf_op jit(solution)/shard_map/all_to_all | solution.py:98
  37.5 0.5 broadcast.245
  38.0 0.6 reduce.23
  39.1 1.3 all-to-all-done.3
  40.4 5.7 %all-to-all-start.2 = ((bf16[128,4,128]{2,0,1:T(8,128)(2,1)}), bf16[128,4,128]{2,0,1:T(8,128)(2,1)S(1)}, u32[]{:S(2)}, u32[]{:S(2)}) async-start(bf16[128,4,128]{2,0,1:T(8,128)(2,1)} %copy_bitcast_fusion.1), calls=%async_computation.2 | async-start | bytes 262144 | tf_op jit(solution)/shard_map/all_to_all | solution.py:92
  46.0 0.6 reduce.25
  46.9 2.4 %all-to-all-done.2 = bf16[128,4,128]{2,0,1:T(8,128)(2,1)S(1)} async-done(((bf16[128,4,128]{2,0,1:T(8,128)(2,1)}), bf16[128,4,128]{2,0,1:T(8,128)(2,1)S(1)}, u32[]{:S(2)}, u32[]{:S(2)}) %all-to-all-start.2) | async-done | bytes 131104 | tf_op jit(solution)/shard_map/all_to_all | solution.py:92
  49.3 6.0 %all-to-all-start.4 = ((bf16[128,4,128]{2,0,1:T(8,128)(2,1)}), bf16[128,4,128]{2,0,1:T(8,128)(2,1)S(1)}, u32[]{:S(2)}, u32[]{:S(2)}) async-start(bf16[128,4,128]{2,0,1:T(8,128)(2,1)} %copy_bitcast_fusion), calls=%async_computation.4 | async-start | bytes 262144 | tf_op jit(solution)/shard_map/all_to_all | solution.py:92
  55.6 0.7 fusion.6
  56.3 39.3 %custom-call.4 = f32[8,1,64,64]{2,3,1,0:T(8,128)S(1)} custom-call(f32[8,1,64,64]{3,2,1,0:T(8,128)S(1)} %fusion.6), custom_call_target="InvertDiagBlocksLowerTriangular" | custom-call | tf_op jit(solution)/shard_map/jit(_solve_triangular)/vmap()/triangular_solve | solution.py:18
  95.6 4.8 %all-to-all-start.1 = ((bf16[128,4,128]{2,0,1:T(8,128)(2,1)}), bf16[128,4,128]{2,0,1:T(8,128)(2,1)S(1)}, u32[]{:S(2)}, u32[]{:S(2)}) async-start(bf16[128,4,128]{2,0,1:T(8,128)(2,1)} %copy.60), calls=%async_computation.1 | async-start | bytes 262144 | tf_op jit(solution)/shard_map/all_to_all | solution.py:92
  100.8 0.7 convolution_bitcast_fusion.1
  101.5 1.2 fusion.38
  102.7 1.2 convolution_subtract_fusion
  103.8 0.6 convolution_add_fusion.2
  104.6 0.7 fusion.13
  105.3 0.6 convolution_add_fusion.1
  106.0 0.7 fusion.20
  106.6 0.6 convolution_add_fusion
  107.3 0.7 fusion.23
  108.0 1.3 collective-permute-start
  109.3 4.8 %all-to-all-start.5 = ((bf16[128,4,128]{0,2,1:T(8,128)(2,1)}), bf16[128,4,128]{0,2,1:T(8,128)(2,1)S(1)}, u32[]{:S(2)}, u32[]{:S(2)}) async-start(bf16[128,4,128]{0,2,1:T(8,128)(2,1)} %bitcast.67), calls=%async_computation.5 | async-start | bytes 262144 | tf_op jit(solution)/shard_map/all_to_all | solution.py:92
  114.4 0.7 convolution_multiply_fusion.1
  115.5 3.6 %collective-permute-start.1 = (f32[2,1,128,128]{3,2,1,0:T(8,128)S(1)}, f32[2,1,128,128]{3,2,1,0:T(8,128)S(1)}, u32[]{:S(2)}, u32[]{:S(2)}) collective-permute-start(f32[2,1,128,128]{3,2,1,0:T(8,128)S(1)} %pad_maximum_fusion.3), channel_id=1, source_target_pairs={{0,8},{4,12},{8,16},{12,20},{16,24},{20,28},{24,32},{28,36},{32,40... | collective-permute-start | bytes 393224 | tf_op jit(solution)/shard_map/ppermute | solution.py:132
  119.2 0.4 convolution_subtract_fusion.1
  119.6 2.2 collective-permute-done.1
  122.3 12.9 %collective-permute-start.2 = (f32[2,1,128,128]{3,2,1,0:T(8,128)S(1)}, f32[2,1,128,128]{3,2,1,0:T(8,128)S(1)}, u32[]{:S(2)}, u32[]{:S(2)}) collective-permute-start(f32[2,1,128,128]{3,2,1,0:T(8,128)S(1)} %pad_maximum_fusion.4), channel_id=1, source_target_pairs={{0,16},{4,20},{8,24},{12,28},{16,32},{20,36},{24,40},{28,44},{32,4... | collective-permute-start | bytes 393224 | tf_op jit(solution)/shard_map/ppermute | solution.py:132
  135.3 3.5 %collective-permute-done.2 = f32[2,1,128,128]{3,2,1,0:T(8,128)S(1)} collective-permute-done((f32[2,1,128,128]{3,2,1,0:T(8,128)S(1)}, f32[2,1,128,128]{3,2,1,0:T(8,128)S(1)}, u32[]{:S(2)}, u32[]{:S(2)}) %collective-permute-start.2) | collective-permute-done | bytes 131104 | tf_op jit(solution)/shard_map/ppermute | solution.py:132
  139.0 21.5 %collective-permute-start.3 = (f32[1,128,128]{2,1,0:T(8,128)S(1)}, f32[1,128,128]{2,1,0:T(8,128)S(1)}, u32[]{:S(2)}, u32[]{:S(2)}) collective-permute-start(f32[1,128,128]{2,1,0:T(8,128)S(1)} %bitcast.226), channel_id=1, source_target_pairs={{0,32},{4,36},{8,40},{12,44},{16,48},{20,52},{24,56},{28,60},{1,33... | collective-permute-start | bytes 196616 | tf_op jit(solution)/shard_map/ppermute | solution.py:139
  160.7 1.9 collective-permute-done.3
  162.9 1.3 collective-permute-start.4
  164.2 1.8 collective-permute-done.4
  166.0 0.6 fusion.1
  166.6 0.6 fusion.75
  167.2 0.5 multiply_reduce_fusion
  168.1 10.0 %all_to_all.94 = bf16[4,128,128]{1,2,0:T(8,128)(2,1)S(1)} all-to-all(bf16[4,128,128]{1,2,0:T(8,128)(2,1)S(1)} %fusion.45), channel_id=1, replica_groups=mesh['heads'=8,'z'=16,'x'=4] {'x'}, dimensions={0} | all-to-all | bytes 262144 | tf_op jit(solution)/shard_map/all_to_all | solution.py:155
  178.1 4.7 %convolution_convert_fusion = bf16[128,4096]{1,0:T(8,128)(2,1)} fusion(bf16[128,512]{0,1:T(8,128)(2,1)S(1)} %bitcast.223, bf16[512,4096]{0,1:T(8,128)(2,1)} %all-gather.3.cloned.1.call-done), kind=kOutput, calls=%fused_computation | convolution fusion | flops 537395200 | bytes 5373952 | tf_op jit(solution)/shard_map/dot_general | solution.py:156
  182.8 45.0 %reduce-scatter.2.cloned.1.call-done = bf16[128,512]{1,0:T(8,128)(2,1)} async-done(((bf16[128,4096]{1,0:T(8,128)(2,1)}), bf16[128,512]{1,0:T(8,128)(2,1)}) %reduce-scatter.2.cloned.1.call-update) | async-done | bytes 131088 | tf_op jit(solution)/shard_map/reduce_scatter | solution.py:161
  (66 shorter events, 4.4 us)
Async XLA Ops:
  6.5 10.0 %copy-start = (bf16[128,512]{1,0:T(8,128)(2,1)S(1)}, bf16[128,512]{1,0:T(8,128)(2,1)}, u32[]{:S(2)}) copy-start(bf16[128,512]{1,0:T(8,128)(2,1)} %param.10) | copy-start | bytes 393220
  6.5 25.1 %all-to-all-start = ((f32[4,1,128]{2,1,0:T(1,128)}), f32[4,1,128]{2,1,0:T(1,128)S(1)}, u32[]{:S(2)}, u32[]{:S(2)}) async-start(f32[4,1,128]{2,1,0:T(1,128)} %bitcast.231), calls=%async_computation | async-start | bytes 4096 | tf_op jit(solution)/shard_map/all_to_all | solution.py:99
  15.7 162.4 %all-gather.3.cloned.1.call-start = ((), (), s32[]{:S(2)}) async-start(), calls=%async_computation.8 | async-start | bytes 4259840 | tf_op jit(solution)/shard_map/all_gather | solution.py:158
  31.6 8.8 %all-to-all-start.3 = ((f32[4,1,128]{2,1,0:T(1,128)}), f32[4,1,128]{2,1,0:T(1,128)S(1)}, u32[]{:S(2)}, u32[]{:S(2)}) async-start(f32[4,1,128]{2,1,0:T(1,128)} %bitcast.232), calls=%async_computation.3 | async-start | bytes 4096 | tf_op jit(solution)/shard_map/all_to_all | solution.py:98
  40.4 8.9 %all-to-all-start.2 = ((bf16[128,4,128]{2,0,1:T(8,128)(2,1)}), bf16[128,4,128]{2,0,1:T(8,128)(2,1)S(1)}, u32[]{:S(2)}, u32[]{:S(2)}) async-start(bf16[128,4,128]{2,0,1:T(8,128)(2,1)} %copy_bitcast_fusion.1), calls=%async_computation.2 | async-start | bytes 262144 | tf_op jit(solution)/shard_map/all_to_all | solution.py:92
  49.3 46.3 %all-to-all-start.4 = ((bf16[128,4,128]{2,0,1:T(8,128)(2,1)}), bf16[128,4,128]{2,0,1:T(8,128)(2,1)S(1)}, u32[]{:S(2)}, u32[]{:S(2)}) async-start(bf16[128,4,128]{2,0,1:T(8,128)(2,1)} %copy_bitcast_fusion), calls=%async_computation.4 | async-start | bytes 262144 | tf_op jit(solution)/shard_map/all_to_all | solution.py:92
  95.6 13.7 %all-to-all-start.1 = ((bf16[128,4,128]{2,0,1:T(8,128)(2,1)}), bf16[128,4,128]{2,0,1:T(8,128)(2,1)S(1)}, u32[]{:S(2)}, u32[]{:S(2)}) async-start(bf16[128,4,128]{2,0,1:T(8,128)(2,1)} %copy.60), calls=%async_computation.1 | async-start | bytes 262144 | tf_op jit(solution)/shard_map/all_to_all | solution.py:92
  108.0 7.1 %collective-permute-start = (f32[2,1,128,128]{3,2,1,0:T(8,128)S(1)}, f32[2,1,128,128]{3,2,1,0:T(8,128)S(1)}, u32[]{:S(2)}, u32[]{:S(2)}) collective-permute-start(f32[2,1,128,128]{3,2,1,0:T(8,128)S(1)} %pad_maximum_fusion.2), channel_id=1, source_target_pairs={{0,4},{4,8},{8,12},{12,16},{16,20},{20,24},{24,28},{28,32},{32,36}... | collective-permute-start | bytes 393224 | tf_op jit(solution)/shard_map/ppermute | solution.py:132
  109.3 58.6 %all-to-all-start.5 = ((bf16[128,4,128]{0,2,1:T(8,128)(2,1)}), bf16[128,4,128]{0,2,1:T(8,128)(2,1)S(1)}, u32[]{:S(2)}, u32[]{:S(2)}) async-start(bf16[128,4,128]{0,2,1:T(8,128)(2,1)} %bitcast.67), calls=%async_computation.5 | async-start | bytes 262144 | tf_op jit(solution)/shard_map/all_to_all | solution.py:92
  114.1 113.7 %reduce-scatter.2.cloned.1.call-start = ((), (), s32[]{:S(2)}) async-start(), calls=%async_computation.9 | async-start | bytes 1179648 | tf_op jit(solution)/shard_map/reduce_scatter | solution.py:161
  115.5 6.3 %collective-permute-start.1 = (f32[2,1,128,128]{3,2,1,0:T(8,128)S(1)}, f32[2,1,128,128]{3,2,1,0:T(8,128)S(1)}, u32[]{:S(2)}, u32[]{:S(2)}) collective-permute-start(f32[2,1,128,128]{3,2,1,0:T(8,128)S(1)} %pad_maximum_fusion.3), channel_id=1, source_target_pairs={{0,8},{4,12},{8,16},{12,20},{16,24},{20,28},{24,32},{28,36},{32,40... | collective-permute-start | bytes 393224 | tf_op jit(solution)/shard_map/ppermute | solution.py:132
  119.2 48.8 %copy-start.1 = (f32[128]{0:T(128)S(1)}, f32[128]{0:T(128)}, u32[]{:S(2)}) copy-start(f32[128]{0:T(128)} %param.16) | copy-start | bytes 1540
  122.3 16.5 %collective-permute-start.2 = (f32[2,1,128,128]{3,2,1,0:T(8,128)S(1)}, f32[2,1,128,128]{3,2,1,0:T(8,128)S(1)}, u32[]{:S(2)}, u32[]{:S(2)}) collective-permute-start(f32[2,1,128,128]{3,2,1,0:T(8,128)S(1)} %pad_maximum_fusion.4), channel_id=1, source_target_pairs={{0,16},{4,20},{8,24},{12,28},{16,32},{20,36},{24,40},{28,44},{32,4... | collective-permute-start | bytes 393224 | tf_op jit(solution)/shard_map/ppermute | solution.py:132
  139.0 23.7 %collective-permute-start.3 = (f32[1,128,128]{2,1,0:T(8,128)S(1)}, f32[1,128,128]{2,1,0:T(8,128)S(1)}, u32[]{:S(2)}, u32[]{:S(2)}) collective-permute-start(f32[1,128,128]{2,1,0:T(8,128)S(1)} %bitcast.226), channel_id=1, source_target_pairs={{0,32},{4,36},{8,40},{12,44},{16,48},{20,52},{24,56},{28,60},{1,33... | collective-permute-start | bytes 196616 | tf_op jit(solution)/shard_map/ppermute | solution.py:139
  162.9 3.2 %collective-permute-start.4 = (f32[1,128,128]{2,1,0:T(8,128)S(1)}, f32[1,128,128]{2,1,0:T(8,128)S(1)}, u32[]{:S(2)}, u32[]{:S(2)}) collective-permute-start(f32[1,128,128]{2,1,0:T(8,128)S(1)} %fusion.7), channel_id=1, source_target_pairs={{0,4},{4,8},{8,12},{12,16},{16,20},{20,24},{24,28},{28,32},{32,36}... | collective-permute-start | bytes 196616 | tf_op jit(solution)/shard_map/ppermute | solution.py:143
Sparse Core Ops, SparseCore 0:
  19.4 151.3 all-gather.2
  182.9 44.7 reduce-scatter.1
where the time goes:
time: 235 us
  starting transfers between devices  77 us (33%)
  waiting for transfers between devices  58.9 us (25%)
  other arithmetic  42.6 us (18%)
  blocking collectives  17.7 us (8%)
  matrix products  16.4 us (7%)
  between operations  13.9 us (6%)
  local copies, waits for them, and re-layouts  8.12 us (3%)
    reduce_scatter x1, waiting for transfers between devices, on_device(): lax.psum_scatter(partial_value.astype(jnp.bfloat16), 'heads', scatter_dim...  45 us
    another operation x2, other arithmetic, triangular_inverse_below(): jax.scipy.linalg.solve_triangular(system, right_side, lower=True, unit_di...  39.3 us
    ppermute x1, starting transfers between devices, on_device(): got_saved = lax.ppermute(group_saved, 'z', pairs)  21.5 us
    all_to_all x4, starting transfers between devices, spread(): return lax.all_to_all(array, 'x', 1, 0, tiled=True)  21.3 us
    ppermute x3, starting transfers between devices, on_device(): got = lax.ppermute(jnp.stack([group_reach, group_saved]), 'z', pairs)  17.9 us
    all_to_all x1, blocking collectives, on_device(): normed = lax.all_to_all(normed, 'x', 0, 1, tiled=True)  10 us
    all_to_all x1, starting transfers between devices, on_device(): decays_here = lax.all_to_all(log_decay, 'x', 0, 1, tiled=True)  9.17 us
    all_gather x1, blocking collectives, on_device(): resets_here = lax.all_gather(doc_start, 'x', tiled=True)  7.65 us
  transfers between devices with their start and end apart: 13, of which 7 were waited for; matrix products, arithmetic and copies ran while one was open for 27% of the time, Pallas kernels for 0%

commit v1 on v0

--- a/solution.py
+++ b/solution.py
@@ -97,7 +97,15 @@
     gate_here = spread(gate_proj)
     rates_here = lax.all_to_all(write_rate, "x", 0, 1, tiled=True)
     decays_here = lax.all_to_all(log_decay, "x", 0, 1, tiled=True)
-    resets_here = lax.all_gather(doc_start, "x", tiled=True)
+    resets_here = jnp.concatenate(
+        lax.all_to_all(
+            jnp.stack([doc_start for _ in range(lax.axis_size("x"))]),
+            axis_name="x",
+            split_axis=0,
+            concat_axis=0,
+        ),
+        axis=0,
+    )
     tok_rows = query_here.shape[0]
     local_heads = head_count // minor
     blocks = tok_rows // STRETCH

time: 235 us -> 232 us (0.987)
  the two profiles are of different devices: /device:TPU:4 before, /device:TPU:2 now
where the time goes in v1:
time: 232 us; the launch traced here: 231 us
  starting transfers between devices  81 us (35%)
  waiting for transfers between devices  59.7 us (26%)
  other arithmetic  42.8 us (18%)
  matrix products  16.4 us (7%)
  between operations  13.9 us (6%)
  local copies, waits for them, and re-layouts  9.43 us (4%)
  blocking collectives  8.28 us (4%)
    reduce_scatter x1, waiting for transfers between devices, on_device(): lax.psum_scatter(partial_value.astype(jnp.bfloat16), 'heads', scatter_dim...  42.9 us
    another operation x2, other arithmetic, triangular_inverse_below(): jax.scipy.linalg.solve_triangular(system, right_side, lower=True, unit_di...  39.3 us
    ppermute x1, starting transfers between devices, on_device(): got_saved = lax.ppermute(group_saved, 'z', pairs)  20 us
    all_to_all x4, starting transfers between devices, spread(): return lax.all_to_all(array, 'x', 1, 0, tiled=True)  19.1 us
    ppermute x3, starting transfers between devices, on_device(): got = lax.ppermute(jnp.stack([group_reach, group_saved]), 'z', pairs)  17.2 us
    all_to_all x1, starting transfers between devices, on_device(): decays_here = lax.all_to_all(log_decay, 'x', 0, 1, tiled=True)  9.2 us
    all_to_all x1, blocking collectives, on_device(): normed = lax.all_to_all(normed, 'x', 0, 1, tiled=True)  8.28 us
    ppermute x1, starting transfers between devices, on_device(): lax.ppermute(group_saved, 'z', [(i, i + 1) for i in range(major - 1)])  6.04 us
  transfers between devices with their start and end apart: 14, of which 8 were waited for; matrix products, arithmetic and copies ran while one was open for 28% of the time, Pallas kernels for 0%

profile of v1, /device:TPU:2, one launch (start us, length us, event | category | flops | bytes accessed | tf_op | source)
XLA Modules:
  0.0 231.5 jit_solution(4127435185701801845)
XLA Ops:
  6.5 9.2 %all-to-all-start.1 = ((f32[4,1,128]{2,1,0:T(1,128)}), f32[4,1,128]{2,1,0:T(1,128)S(1)}, u32[]{:S(2)}, u32[]{:S(2)}) async-start(f32[4,1,128]{2,1,0:T(1,128)} %bitcast.230), calls=%async_computation.1 | async-start | bytes 4096 | tf_op jit(solution)/shard_map/all_to_all | solution.py:99
  15.7 0.7 all-gather.2.cloned.1.call-update
  16.5 0.7 copy_bitcast_fusion.1
  17.3 1.6 copy_bitcast_fusion
  18.8 0.7 all-to-all-done.1
  19.5 1.2 stack.28
  20.7 4.6 %all-to-all-start = ((s32[4,1,128]{2,1,0:T(1,128)}), s32[4,1,128]{2,1,0:T(1,128)S(1)}, u32[]{:S(2)}, u32[]{:S(2)}) async-start(s32[4,1,128]{2,1,0:T(1,128)} %stack.28), calls=%async_computation | async-start | bytes 4096 | tf_op jit(solution)/shard_map/all_to_all | solution.py:101
  25.4 1.0 copy.59
  26.4 0.8 copy.60
  27.2 1.7 copy.69
  28.8 0.6 broadcast.249
  29.4 0.7 reduce.23
  30.2 4.8 %all-to-all-start.4 = ((f32[4,1,128]{2,1,0:T(1,128)}), f32[4,1,128]{2,1,0:T(1,128)S(1)}, u32[]{:S(2)}, u32[]{:S(2)}) async-start(f32[4,1,128]{2,1,0:T(1,128)} %bitcast.231), calls=%async_computation.4 | async-start | bytes 4096 | tf_op jit(solution)/shard_map/all_to_all | solution.py:98
  35.0 0.5 broadcast.250
  35.5 0.6 reduce.24
  36.9 1.8 all-to-all-done.4
  38.7 4.7 %all-to-all-start.3 = ((bf16[128,4,128]{2,0,1:T(8,128)(2,1)}), bf16[128,4,128]{2,0,1:T(8,128)(2,1)S(1)}, u32[]{:S(2)}, u32[]{:S(2)}) async-start(bf16[128,4,128]{2,0,1:T(8,128)(2,1)} %copy_bitcast_fusion.1), calls=%async_computation.3 | async-start | bytes 262144 | tf_op jit(solution)/shard_map/all_to_all | solution.py:92
  43.5 0.7 reduce.25
  44.5 4.1 %all-to-all-done.3 = bf16[128,4,128]{2,0,1:T(8,128)(2,1)S(1)} async-done(((bf16[128,4,128]{2,0,1:T(8,128)(2,1)}), bf16[128,4,128]{2,0,1:T(8,128)(2,1)S(1)}, u32[]{:S(2)}, u32[]{:S(2)}) %all-to-all-start.3) | async-done | bytes 131104 | tf_op jit(solution)/shard_map/all_to_all | solution.py:92
  48.6 4.7 %all-to-all-start.5 = ((bf16[128,4,128]{2,0,1:T(8,128)(2,1)}), bf16[128,4,128]{2,0,1:T(8,128)(2,1)S(1)}, u32[]{:S(2)}, u32[]{:S(2)}) async-start(bf16[128,4,128]{2,0,1:T(8,128)(2,1)} %copy_bitcast_fusion), calls=%async_computation.5 | async-start | bytes 262144 | tf_op jit(solution)/shard_map/all_to_all | solution.py:92
  53.6 0.7 fusion.6
  54.3 39.3 %custom-call.4 = f32[8,1,64,64]{2,3,1,0:T(8,128)S(1)} custom-call(f32[8,1,64,64]{3,2,1,0:T(8,128)S(1)} %fusion.6), custom_call_target="InvertDiagBlocksLowerTriangular" | custom-call | tf_op jit(solution)/shard_map/jit(_solve_triangular)/vmap()/triangular_solve | solution.py:18
  93.7 4.8 %all-to-all-start.2 = ((bf16[128,4,128]{2,0,1:T(8,128)(2,1)}), bf16[128,4,128]{2,0,1:T(8,128)(2,1)S(1)}, u32[]{:S(2)}, u32[]{:S(2)}) async-start(bf16[128,4,128]{2,0,1:T(8,128)(2,1)} %copy.60), calls=%async_computation.2 | async-start | bytes 262144 | tf_op jit(solution)/shard_map/all_to_all | solution.py:92
  98.8 0.7 convolution_bitcast_fusion.1
  99.5 1.2 fusion.38
  100.7 1.2 convolution_subtract_fusion
  101.9 0.6 convolution_add_fusion.2
  102.6 0.7 fusion.13
  103.3 0.6 convolution_add_fusion.1
  104.0 0.7 fusion.20
  104.7 0.6 convolution_add_fusion
  105.3 0.7 fusion.23
  106.0 1.3 collective-permute-start
  107.3 4.8 %all-to-all-start.6 = ((bf16[128,4,128]{0,2,1:T(8,128)(2,1)}), bf16[128,4,128]{0,2,1:T(8,128)(2,1)S(1)}, u32[]{:S(2)}, u32[]{:S(2)}) async-start(bf16[128,4,128]{0,2,1:T(8,128)(2,1)} %bitcast.66), calls=%async_computation.6 | async-start | bytes 262144 | tf_op jit(solution)/shard_map/all_to_all | solution.py:92
  112.4 0.7 convolution_multiply_fusion.1
  113.6 3.2 %collective-permute-start.1 = (f32[2,1,128,128]{3,2,1,0:T(8,128)S(1)}, f32[2,1,128,128]{3,2,1,0:T(8,128)S(1)}, u32[]{:S(2)}, u32[]{:S(2)}) collective-permute-start(f32[2,1,128,128]{3,2,1,0:T(8,128)S(1)} %pad_maximum_fusion.3), channel_id=1, source_target_pairs={{0,8},{4,12},{8,16},{12,20},{16,24},{20,28},{24,32},{28,36},{32,40... | collective-permute-start | bytes 393224 | tf_op jit(solution)/shard_map/ppermute | solution.py:140
  117.2 2.2 collective-permute-done.1
  119.8 12.8 %collective-permute-start.2 = (f32[2,1,128,128]{3,2,1,0:T(8,128)S(1)}, f32[2,1,128,128]{3,2,1,0:T(8,128)S(1)}, u32[]{:S(2)}, u32[]{:S(2)}) collective-permute-start(f32[2,1,128,128]{3,2,1,0:T(8,128)S(1)} %pad_maximum_fusion.4), channel_id=1, source_target_pairs={{0,16},{4,20},{8,24},{12,28},{16,32},{20,36},{24,40},{28,44},{32,4... | collective-permute-start | bytes 393224 | tf_op jit(solution)/shard_map/ppermute | solution.py:140
  132.7 3.1 %collective-permute-done.2 = f32[2,1,128,128]{3,2,1,0:T(8,128)S(1)} collective-permute-done((f32[2,1,128,128]{3,2,1,0:T(8,128)S(1)}, f32[2,1,128,128]{3,2,1,0:T(8,128)S(1)}, u32[]{:S(2)}, u32[]{:S(2)}) %collective-permute-start.2) | collective-permute-done | bytes 131104 | tf_op jit(solution)/shard_map/ppermute | solution.py:140
  136.0 20.0 %collective-permute-start.3 = (f32[1,128,128]{2,1,0:T(8,128)S(1)}, f32[1,128,128]{2,1,0:T(8,128)S(1)}, u32[]{:S(2)}, u32[]{:S(2)}) collective-permute-start(f32[1,128,128]{2,1,0:T(8,128)S(1)} %bitcast.225), channel_id=1, source_target_pairs={{0,32},{4,36},{8,40},{12,44},{16,48},{20,52},{24,56},{28,60},{1,33... | collective-permute-start | bytes 196616 | tf_op jit(solution)/shard_map/ppermute | solution.py:147
  156.2 2.1 collective-permute-done.3
  158.6 6.0 %collective-permute-start.4 = (f32[1,128,128]{2,1,0:T(8,128)S(1)}, f32[1,128,128]{2,1,0:T(8,128)S(1)}, u32[]{:S(2)}, u32[]{:S(2)}) collective-permute-start(f32[1,128,128]{2,1,0:T(8,128)S(1)} %fusion.7), channel_id=1, source_target_pairs={{0,4},{4,8},{8,12},{12,16},{16,20},{20,24},{24,28},{28,32},{32,36}... | collective-permute-start | bytes 196616 | tf_op jit(solution)/shard_map/ppermute | solution.py:151
  164.7 2.1 collective-permute-done.4
  166.7 0.6 fusion.1
  167.3 0.6 fusion.75
  168.8 8.3 %all_to_all.100 = bf16[4,128,128]{1,2,0:T(8,128)(2,1)S(1)} all-to-all(bf16[4,128,128]{1,2,0:T(8,128)(2,1)S(1)} %fusion.45), channel_id=1, replica_groups=mesh['heads'=8,'z'=16,'x'=4] {'x'}, dimensions={0} | all-to-all | bytes 262144 | tf_op jit(solution)/shard_map/all_to_all | solution.py:163
  177.1 4.7 %convolution_convert_fusion = bf16[128,4096]{1,0:T(8,128)(2,1)} fusion(bf16[128,512]{0,1:T(8,128)(2,1)S(1)} %bitcast.222, bf16[512,4096]{0,1:T(8,128)(2,1)} %all-gather.2.cloned.1.call-done), kind=kOutput, calls=%fused_computation | convolution fusion | flops 537395200 | bytes 5373952 | tf_op jit(solution)/shard_map/dot_general | solution.py:164
  181.8 42.9 %reduce-scatter.2.cloned.1.call-done = bf16[128,512]{1,0:T(8,128)(2,1)} async-done(((bf16[128,4096]{1,0:T(8,128)(2,1)}), bf16[128,512]{1,0:T(8,128)(2,1)}) %reduce-scatter.2.cloned.1.call-update) | async-done | bytes 131088 | tf_op jit(solution)/shard_map/reduce_scatter | solution.py:169
  (68 shorter events, 5.3 us)
Async XLA Ops:
  6.5 10.0 %copy-start = (bf16[128,512]{1,0:T(8,128)(2,1)S(1)}, bf16[128,512]{1,0:T(8,128)(2,1)}, u32[]{:S(2)}) copy-start(bf16[128,512]{1,0:T(8,128)(2,1)} %param.10) | copy-start | bytes 393220
  6.5 13.0 %all-to-all-start.1 = ((f32[4,1,128]{2,1,0:T(1,128)}), f32[4,1,128]{2,1,0:T(1,128)S(1)}, u32[]{:S(2)}, u32[]{:S(2)}) async-start(f32[4,1,128]{2,1,0:T(1,128)} %bitcast.230), calls=%async_computation.1 | async-start | bytes 4096 | tf_op jit(solution)/shard_map/all_to_all | solution.py:99
  15.7 161.3 %all-gather.2.cloned.1.call-start = ((), (), s32[]{:S(2)}) async-start(), calls=%async_computation.9 | async-start | bytes 4259840 | tf_op jit(solution)/shard_map/all_gather | solution.py:166
  20.7 9.4 %all-to-all-start = ((s32[4,1,128]{2,1,0:T(1,128)}), s32[4,1,128]{2,1,0:T(1,128)S(1)}, u32[]{:S(2)}, u32[]{:S(2)}) async-start(s32[4,1,128]{2,1,0:T(1,128)} %stack.28), calls=%async_computation | async-start | bytes 4096 | tf_op jit(solution)/shard_map/all_to_all | solution.py:101
  30.2 8.6 %all-to-all-start.4 = ((f32[4,1,128]{2,1,0:T(1,128)}), f32[4,1,128]{2,1,0:T(1,128)S(1)}, u32[]{:S(2)}, u32[]{:S(2)}) async-start(f32[4,1,128]{2,1,0:T(1,128)} %bitcast.231), calls=%async_computation.4 | async-start | bytes 4096 | tf_op jit(solution)/shard_map/all_to_all | solution.py:98
  38.7 9.9 %all-to-all-start.3 = ((bf16[128,4,128]{2,0,1:T(8,128)(2,1)}), bf16[128,4,128]{2,0,1:T(8,128)(2,1)S(1)}, u32[]{:S(2)}, u32[]{:S(2)}) async-start(bf16[128,4,128]{2,0,1:T(8,128)(2,1)} %copy_bitcast_fusion.1), calls=%async_computation.3 | async-start | bytes 262144 | tf_op jit(solution)/shard_map/all_to_all | solution.py:92
  48.6 45.1 %all-to-all-start.5 = ((bf16[128,4,128]{2,0,1:T(8,128)(2,1)}), bf16[128,4,128]{2,0,1:T(8,128)(2,1)S(1)}, u32[]{:S(2)}, u32[]{:S(2)}) async-start(bf16[128,4,128]{2,0,1:T(8,128)(2,1)} %copy_bitcast_fusion), calls=%async_computation.5 | async-start | bytes 262144 | tf_op jit(solution)/shard_map/all_to_all | solution.py:92
  93.7 13.7 %all-to-all-start.2 = ((bf16[128,4,128]{2,0,1:T(8,128)(2,1)}), bf16[128,4,128]{2,0,1:T(8,128)(2,1)S(1)}, u32[]{:S(2)}, u32[]{:S(2)}) async-start(bf16[128,4,128]{2,0,1:T(8,128)(2,1)} %copy.60), calls=%async_computation.2 | async-start | bytes 262144 | tf_op jit(solution)/shard_map/all_to_all | solution.py:92
  106.0 7.1 %collective-permute-start = (f32[2,1,128,128]{3,2,1,0:T(8,128)S(1)}, f32[2,1,128,128]{3,2,1,0:T(8,128)S(1)}, u32[]{:S(2)}, u32[]{:S(2)}) collective-permute-start(f32[2,1,128,128]{3,2,1,0:T(8,128)S(1)} %pad_maximum_fusion.2), channel_id=1, source_target_pairs={{0,4},{4,8},{8,12},{12,16},{16,20},{20,24},{24,28},{28,32},{32,36}... | collective-permute-start | bytes 393224 | tf_op jit(solution)/shard_map/ppermute | solution.py:140
  107.3 61.3 %all-to-all-start.6 = ((bf16[128,4,128]{0,2,1:T(8,128)(2,1)}), bf16[128,4,128]{0,2,1:T(8,128)(2,1)S(1)}, u32[]{:S(2)}, u32[]{:S(2)}) async-start(bf16[128,4,128]{0,2,1:T(8,128)(2,1)} %bitcast.66), calls=%async_computation.6 | async-start | bytes 262144 | tf_op jit(solution)/shard_map/all_to_all | solution.py:92
  112.2 112.5 %reduce-scatter.2.cloned.1.call-start = ((), (), s32[]{:S(2)}) async-start(), calls=%async_computation.10 | async-start | bytes 1179648 | tf_op jit(solution)/shard_map/reduce_scatter | solution.py:169
  113.6 5.8 %collective-permute-start.1 = (f32[2,1,128,128]{3,2,1,0:T(8,128)S(1)}, f32[2,1,128,128]{3,2,1,0:T(8,128)S(1)}, u32[]{:S(2)}, u32[]{:S(2)}) collective-permute-start(f32[2,1,128,128]{3,2,1,0:T(8,128)S(1)} %pad_maximum_fusion.3), channel_id=1, source_target_pairs={{0,8},{4,12},{8,16},{12,20},{16,24},{20,28},{24,32},{28,36},{32,40... | collective-permute-start | bytes 393224 | tf_op jit(solution)/shard_map/ppermute | solution.py:140
  116.8 51.9 %copy-start.1 = (f32[128]{0:T(128)S(1)}, f32[128]{0:T(128)}, u32[]{:S(2)}) copy-start(f32[128]{0:T(128)} %param.16) | copy-start | bytes 1540
  119.8 15.9 %collective-permute-start.2 = (f32[2,1,128,128]{3,2,1,0:T(8,128)S(1)}, f32[2,1,128,128]{3,2,1,0:T(8,128)S(1)}, u32[]{:S(2)}, u32[]{:S(2)}) collective-permute-start(f32[2,1,128,128]{3,2,1,0:T(8,128)S(1)} %pad_maximum_fusion.4), channel_id=1, source_target_pairs={{0,16},{4,20},{8,24},{12,28},{16,32},{20,36},{24,40},{28,44},{32,4... | collective-permute-start | bytes 393224 | tf_op jit(solution)/shard_map/ppermute | solution.py:140
  136.0 22.4 %collective-permute-start.3 = (f32[1,128,128]{2,1,0:T(8,128)S(1)}, f32[1,128,128]{2,1,0:T(8,128)S(1)}, u32[]{:S(2)}, u32[]{:S(2)}) collective-permute-start(f32[1,128,128]{2,1,0:T(8,128)S(1)} %bitcast.225), channel_id=1, source_target_pairs={{0,32},{4,36},{8,40},{12,44},{16,48},{20,52},{24,56},{28,60},{1,33... | collective-permute-start | bytes 196616 | tf_op jit(solution)/shard_map/ppermute | solution.py:147
  158.6 8.2 %collective-permute-start.4 = (f32[1,128,128]{2,1,0:T(8,128)S(1)}, f32[1,128,128]{2,1,0:T(8,128)S(1)}, u32[]{:S(2)}, u32[]{:S(2)}) collective-permute-start(f32[1,128,128]{2,1,0:T(8,128)S(1)} %fusion.7), channel_id=1, source_target_pairs={{0,4},{4,8},{8,12},{12,16},{16,20},{20,24},{24,28},{28,32},{32,36}... | collective-permute-start | bytes 196616 | tf_op jit(solution)/shard_map/ppermute | solution.py:151
Sparse Core Ops, SparseCore 0:
  19.5 150.8 all-gather.1
  181.9 42.6 reduce-scatter.1
